TPU v7x, 128 devices: a whole 4x4x4 slice. The times are simulated.
128 devices in a mesh: req: 64 (over z, y, x), col: 2 (over core).
Axes of the slice: x: 4, y: 4, z: 4, core: 2. Of those that a mesh axis runs over, the one named last changes fastest.
Arguments:
- tokens: bfloat16 [32768, 1024], P(('req', 'col')), may hold values from -6 to 6
- norm_gain_pair: float32 [2, 1024], replicated, may hold values from 0.5 to 1.5
- query_key_value_weight: bfloat16 [3, 1024, 1024], P(None, None, 'col'), may hold values from -1 to 1
- head_gate_weight: bfloat16 [2, 1024, 8], P(None, None, 'col'), may hold values from -0.1875 to 0.1875
- decay_logit_bias: float32 [8], P('col'), may hold values from -1 to 1024, as said below
- adapter_down_factor: bfloat16 [64, 1024, 16], P('col'), may hold values from -0.1875 to 0.1875
- adapter_up_factor: bfloat16 [64, 16, 1024], P(None, None, 'col'), may hold values from -1.5 to 1.5
- lengths: int32 [64, 2, 3], P('req'), may hold values from 1 to 128, 256 in all within a row
- request_adapter_index: int32 [64, 6], P('req'), may hold values from 0 to 63
- request_cache_index: int32 [64, 6], P('req'), may hold values from 0 to 511
- caches: bfloat16 [256, 8, 128, 128], P('req', 'col'), may hold values from -6 to 6
- head_output_weight: bfloat16 [1024, 1024], P('col'), may hold values from -0.1875 to 0.1875
- feedforward_weight: bfloat16 [3, 1024, 2816], P(None, None, 'col'), may hold values from -0.1875 to 0.1875
Outputs:
- layer_out: bfloat16 [32768, 1024], P(('req', 'col'))
Inputs may be any that keep to these rules, and one draw needn't show every extreme that they name: The 3 lengths of one device sum to 256, and the longest of them is exactly 128. `request_cache_index`: a value of 256 or more means that the request has no cached memory state. `decay_logit_bias`: at most the logarithm of 512.
All inputs are finite; a program needn't handle non-finite values.
Results may differ from a plain program's by a relative error of at most 0.015.
Values may be sent and summed in bfloat16 or wider, within the bound.
No kernel may reach another device: no remote copies, remote signals or barrier semaphores. Data moves between devices by JAX's collectives and lax.ppermute only.
A program may use at most 192 MiB of HBM per device.

v0:
```python
import math
import jax
import jax.numpy as jnp
from jax import lax
from jax.sharding import PartitionSpec as P

epsilon = 1e-05


def rms_scale(values, gain):
    widened = values.astype(jnp.float32)
    factor = lax.rsqrt(jnp.mean(widened * widened, axis=-1, keepdims=True) + epsilon)
    return (widened * factor * gain).astype(jnp.bfloat16)


def on_device(
    tokens,
    norm_gain_pair,
    query_key_value_weight,
    head_gate_weight,
    decay_logit_bias,
    adapter_down_factor,
    adapter_up_factor,
    lengths,
    request_adapter_index,
    request_cache_index,
    caches,
    head_output_weight,
    feedforward_weight,
):
    tok_rows, width = tokens.shape
    col_count = lax.axis_size("col")
    group = tok_rows * col_count
    head_cols = query_key_value_weight.shape[2]
    local_heads = head_gate_weight.shape[2]
    head_size = head_cols // local_heads
    group_lengths = lengths[0].reshape(-1)
    scale = 1.0 / math.sqrt(head_size)
    normalized_rows = rms_scale(tokens, norm_gain_pair[0])
    gathered = lax.all_gather(normalized_rows, "col", axis=0, tiled=True)
    positions = jnp.arange(group, dtype=jnp.int32)
    ends = jnp.cumsum(group_lengths)
    starts = ends - group_lengths
    member = (
        (positions[:, None] >= starts[None, :]) & (positions[:, None] < ends[None, :])
    ).astype(jnp.float32)
    segment = jnp.sum((positions[:, None] >= ends[None, :]).astype(jnp.int32), axis=1)
    projected = jnp.einsum(
        "td,kdc->ktc", gathered, query_key_value_weight, preferred_element_type=jnp.float32
    )
    token_segment = lax.all_gather(adapter_down_factor, "col", axis=0, tiled=True)
    numbers = jnp.arange(token_segment.shape[0], dtype=jnp.int32)
    select = (request_adapter_index[0][:, None] == numbers[None, :]).astype(jnp.bfloat16)
    chosen = jnp.einsum(
        "sa,adr->sdr", select, token_segment, preferred_element_type=jnp.float32
    ).astype(jnp.bfloat16)
    per_request = jnp.einsum("td,sdr->tsr", gathered, chosen, preferred_element_type=jnp.float32)
    low_rank_delta = jnp.sum(member[:, :, None] * per_request, axis=1)
    low_rank_delta = low_rank_delta.astype(jnp.bfloat16)
    adapter_onehot = (
        request_adapter_index[0][:, None]
        == jnp.arange(adapter_up_factor.shape[0], dtype=jnp.int32)[None, :]
    ).astype(jnp.bfloat16)
    up_chosen = jnp.einsum(
        "gq,qjl->gjl", adapter_onehot, adapter_up_factor, preferred_element_type=jnp.float32
    ).astype(jnp.bfloat16)
    delta_all = jnp.einsum(
        "tr,src->tsc", low_rank_delta, up_chosen, preferred_element_type=jnp.float32
    )
    delta = jnp.sum(member[:, :, None] * delta_all, axis=1)
    queries = (projected[0] + delta).astype(jnp.bfloat16).reshape(group, local_heads, head_size)
    keys = projected[1].astype(jnp.bfloat16).reshape(group, local_heads, head_size)
    values = projected[2].astype(jnp.bfloat16).reshape(group, local_heads, head_size)
    gate_terms = jnp.einsum(
        "td,kdh->kth", gathered, head_gate_weight, preferred_element_type=jnp.float32
    )
    log_keep = jax.nn.log_sigmoid(gate_terms[0] + decay_logit_bias[None, :])
    mix_gate = jax.nn.sigmoid(gate_terms[1])
    running = jnp.cumsum(log_keep, axis=0)
    before = running - log_keep
    start_hot = (positions[None, :] == starts[:, None]).astype(jnp.float32)
    start_level = jnp.sum(start_hot[:, :, None] * before[None, :, :], axis=1)
    level = running - jnp.sum(member[:, :, None] * start_level[None, :, :], axis=1)
    token_segment = lax.all_gather(caches, "req", axis=0, tiled=True)
    numbers = jnp.arange(token_segment.shape[0], dtype=jnp.int32)
    select = (request_cache_index[0][:, None] == numbers[None, :]).astype(jnp.bfloat16)
    states = jnp.einsum(
        "sn,nhij->shij", select, token_segment, preferred_element_type=jnp.float32
    ).astype(jnp.bfloat16)
    from_state = jnp.einsum("thi,shij->tshj", queries, states, preferred_element_type=jnp.float32)
    carried = jnp.sum(member[:, :, None, None] * from_state, axis=1) * jnp.exp(level)[:, :, None]
    block = min(512, group)

    def one_block(index):
        begin = index * block
        scores = (
            jnp.einsum("qhd,khd->hqk", queries, keys, preferred_element_type=jnp.float32) * scale
        )
        q_pos = begin + jnp.arange(block, dtype=jnp.int32)
        allowed = (segment[:, None] == segment[None, :]) & (positions[None, :] <= q_pos[:, None])
        masked = jnp.where(allowed[None], scores, -jnp.inf)
        peak = jnp.max(masked, axis=2, keepdims=True)
        weights = jnp.exp(masked - peak)
        probs = (weights / jnp.sum(weights, axis=2, keepdims=True)).astype(jnp.bfloat16)
        attended = jnp.einsum("hqk,khd->qhd", probs, values, preferred_element_type=jnp.float32)
        gap = jnp.where(allowed[None], running.T[:, :, None] - running.T[:, None, :], -jnp.inf)
        memory_w = (scores * jnp.exp(gap)).astype(jnp.bfloat16)
        recalled = jnp.einsum("hqk,khd->qhd", memory_w, values, preferred_element_type=jnp.float32)
        recalled = recalled + carried
        factor = lax.rsqrt(jnp.mean(recalled * recalled, axis=2, keepdims=True) + epsilon)
        combined = attended + mix_gate[:, :, None] * recalled * factor
        return combined.astype(jnp.bfloat16).reshape(block, head_cols)

    blocks = lax.map(one_block, jnp.arange(group // block, dtype=jnp.int32))
    head_out = blocks.reshape(group, head_cols)
    attn_proj = lax.psum_scatter(
        jnp.dot(head_out, head_output_weight, preferred_element_type=jnp.float32),
        "col",
        scatter_dimension=0,
        tiled=True,
    )
    mixed = (tokens.astype(jnp.float32) + attn_proj).astype(jnp.bfloat16)
    normed_two = rms_scale(mixed, norm_gain_pair[1])
    token_segment = lax.all_gather(feedforward_weight, "col", axis=2, tiled=True)
    gate_up = jnp.einsum(
        "td,kdf->ktf", normed_two, token_segment[:2], preferred_element_type=jnp.float32
    )
    hidden = (jax.nn.silu(gate_up[0]) * gate_up[1]).astype(jnp.bfloat16)
    feed = jnp.einsum("tf,df->td", hidden, token_segment[2], preferred_element_type=jnp.float32)
    return (mixed.astype(jnp.float32) + feed).astype(jnp.bfloat16)


def solution(mesh):
    placed = (
        P(("req", "col"), None),
        P(),
        P(None, None, "col"),
        P(None, None, "col"),
        P("col"),
        P("col", None, None),
        P(None, None, "col"),
        P("req", None, None),
        P("req", None),
        P("req", None),
        P("req", "col", None, None),
        P("col", None),
        P(None, None, "col"),
    )
    return jax.shard_map(
        on_device, mesh=mesh, in_specs=placed, out_specs=P(("req", "col"), None), check_vma=False
    )
```

profile of v0, /device:TPU:1, one launch (start us, length us, event | category | flops | bytes accessed | tf_op | source)
XLA Modules:
  0.0 319.6 jit_solution(7090761878730281534)
XLA Ops:
  6.5 1.4 fusion.38
  7.9 1.4 fusion.87
  9.3 2.0 fusion.40
  11.4 0.7 all-gather.7.cloned.1.call-update
  12.1 0.7 all-gather.9.cloned.1.call-update
  12.9 0.8 reshape_squeeze.3
  13.6 0.8 reshape.275
  15.6 2.4 convolution_convert_fusion
  18.1 8.8 %all-gather.5.cloned.1.call-done = bf16[512,1024]{1,0:T(8,128)(2,1)} async-done(((bf16[256,1024]{1,0:T(8,128)(2,1)}), bf16[512,1024]{1,0:T(8,128)(2,1)}) %all-gather.5.cloned.1.call-update) | async-done | bytes 1048592 | tf_op jit(solution)/shard_map/all_gather | solution.py:40
  26.9 1.6 convolution_bitcast_fusion.1
  29.1 1.3 fusion.84
  30.4 1.3 reshape.277
  31.7 3.0 reduce-window.18
  34.8 1.4 slice_reduce_fusion
  36.2 1.3 reduce-window.19
  37.5 0.8 add_bitcast_fusion
  38.9 3.2 %fusion.88 = (bf16[3,512,512]{1,2,0:T(8,128)(2,1)S(1)}, f32[3,512,512]{1,2,0:T(8,128)S(1)}) fusion(bf16[3,1024,512]{2,1,0:T(8,128)(2,1)S(1)} %copy-done, bf16[512,1024]{1,0:T(8,128)(2,1)} %all-gather.5.cloned.1.call-done), kind=kOutput, calls=%fused_computation.113 | convolution fusion | flops 1611399168 | bytes 8912896 | tf_op jit(solution)/shard_map/td,kdc->ktc/dot_general | solution.py:48
  43.7 1.0 fusion.86
  44.8 3.9 %fusion.35 = bf16[6,1024,16]{1,0,2:T(8,128)(2,1)S(1)} fusion(bf16[64,1024,16]{1,2,0:T(8,128)(2,1)} %all-gather.7.cloned.1.call-done, s32[6]{0:T(128)S(1)} %bitcast.135), kind=kOutput, calls=%fused_computation.41 | convolution fusion | flops 12681600 | bytes 2293784 | tf_op jit(solution)/shard_map/sa,adr->sdr/dot_general | solution.py:54
  49.3 1.0 multiply_reduce_fusion
  50.9 4.8 %fusion.89 = (f32[4,512]{1,0:T(4,128)S(1)}, f32[4,512,512]{1,2,0:T(8,128)}) fusion(pred[512,512]{0,1:T(8,128)(4,1)S(1)} %fusion.48, bf16[512,4,128]{0,2,1:T(8,128)(2,1)S(1)} %add_convert_fusion, bf16[512,4,128]{0,2,1:T(8,128)(2,1)} %bitcast.128), kind=kOutput, calls=%fused_computation.114 | convolution fusion | flops 272630272 | bytes 5513216 | tf_op jit(solution)/shard_map/while/body/eval_jaxpr/sub | solution.py:103
  55.7 152.0 %all-gather.9.cloned.1.call-done = bf16[256,4,128,128]{3,2,1,0:T(8,128)(2,1)} async-done(((bf16[4,4,128,128]{3,2,1,0:T(8,128)(2,1)}), bf16[256,4,128,128]{3,2,1,0:T(8,128)(2,1)}) %all-gather.9.cloned.1.call-update) | async-done | bytes 33554448 | tf_op jit(solution)/shard_map/all_gather | solution.py:84
  207.7 32.0 %fusion.20 = bf16[6,4,128,128]{3,0,2,1:T(8,128)(2,1)S(1)} fusion(bf16[256,4,128,128]{3,2,1,0:T(8,128)(2,1)} %all-gather.9.cloned.1.call-done, s32[6]{0:T(128)S(1)} %bitcast.138), kind=kOutput, calls=%fused_computation.33 | convolution fusion | flops 201721344 | bytes 34340888 | tf_op jit(solution)/shard_map/sn,nhij->shij/dot_general | solution.py:87
  239.8 2.0 fusion.5
  241.9 4.1 %multiply_reduce_fusion.1 = (f32[512,4]{0,1:T(4,128)S(1)}, f32[512,4,128]{0,2,1:T(8,128)}) fusion(f32[512,4,128]{0,2,1:T(8,128)} %fusion.5, f32[512,4]{0,1:T(4,128)S(1)} %copy-done.11, bf16[512,4,128]{0,2,1:T(8,128)(2,1)S(1)} %bitcast.126, f32[4,512]{1,0:T(4,128)S(1)} %bitcast.132, pred[512,512]{0,1:T(8,128)(4,1)S(1)} %fusion.48, ...), kind=kOutput, calls=%fused_computation.54 | convolution fusion | flops 543160320 | bytes 3956736 | tf_op jit(solution)/shard_map/while/body/eval_jaxpr/hqk,khd->qhd/dot_general | solution.py:108
  246.0 3.1 fusion.31
  249.1 2.1 fusion.93
  251.8 11.9 %reduce-scatter.2.cloned.1.call-done = f32[256,1024]{1,0:T(8,128)} async-done(((f32[512,1024]{1,0:T(8,128)}), f32[256,1024]{1,0:T(8,128)}) %reduce-scatter.2.cloned.1.call-update) | async-done | bytes 1048592 | tf_op jit(solution)/shard_map/reduce_scatter | solution.py:116
  263.7 1.5 fusion.42
  265.2 36.4 %all-gather.11.cloned.1.call-done = bf16[3,1024,2816]{2,1,0:T(8,128)(2,1)} async-done(((bf16[3,1024,1408]{2,1,0:T(8,128)(2,1)}), bf16[3,1024,2816]{2,1,0:T(8,128)(2,1)}) %all-gather.11.cloned.1.call-update) | async-done | bytes 17301520 | tf_op jit(solution)/shard_map/all_gather | solution.py:124
  301.6 6.1 %fusion.7 = f32[2,256,2816]{2,1,0:T(8,128)S(1)} fusion(bf16[3,1024,2816]{2,1,0:T(8,128)(2,1)} %all-gather.11.cloned.1.call-done, bf16[256,1024]{1,0:T(8,128)(2,1)S(1)} %get-tuple-element.24, f32[1024]{0:T(1024)S(1)} %bitcast.133, f32[256]{0:T(256)S(1)} %add_rsqrt_fusion.1), kind=kOutput, calls=%fused_computation.10 | convolution fusion | flops 2953838592 | bytes 17830912 | tf_op jit(solution)/shard_map/td,kdf->ktf/dot_general | solution.py:125
  307.7 5.4 %fusion.32 = bf16[256,1024]{1,0:T(8,128)(2,1)} fusion(bf16[3,1024,2816]{2,1,0:T(8,128)(2,1)} %all-gather.11.cloned.1.call-done, f32[2,256,2816]{2,1,0:T(8,128)S(1)} %fusion.7, bf16[256,1024]{1,0:T(8,128)(2,1)} %copy-done.7), kind=kOutput, calls=%fused_computation.40 | convolution fusion | flops 1481506816 | bytes 12582912 | tf_op jit(solution)/shard_map/tf,df->td/dot_general | solution.py:129
  (66 shorter events, 6.0 us)
Async XLA Ops:
  6.5 32.3 %copy-start = (bf16[3,1024,512]{2,1,0:T(8,128)(2,1)S(1)}, bf16[3,1024,512]{2,1,0:T(8,128)(2,1)}, u32[]{:S(2)}) copy-start(bf16[3,1024,512]{2,1,0:T(8,128)(2,1)} %param.15) | copy-start | bytes 9437188
  6.5 20.3 %all-gather.5.cloned.1.call-start = ((), (), s32[]{:S(2)}) async-start(), calls=%async_computation.1 | async-start | bytes 1572864 | tf_op jit(solution)/shard_map/all_gather | solution.py:40
  11.3 33.5 %all-gather.7.cloned.1.call-start = ((), (), s32[]{:S(2)}) async-start(), calls=%async_computation.2 | async-start | bytes 3145728 | tf_op jit(solution)/shard_map/all_gather | solution.py:51
  12.1 195.6 %all-gather.9.cloned.1.call-start = ((), (), s32[]{:S(2)}) async-start(), calls=%async_computation.3 | async-start | bytes 34078720 | tf_op jit(solution)/shard_map/all_gather | solution.py:84
  12.8 250.9 %reduce-scatter.2.cloned.1.call-start = ((), (), s32[]{:S(2)}) async-start(), calls=%async_computation.4 | async-start | bytes 3145728 | tf_op jit(solution)/shard_map/reduce_scatter | solution.py:116
  28.5 0.6 copy-start.8
  38.9 3.4 %copy-start.9 = (f32[2,512,4]{1,2,0:T(4,128)S(1)}, f32[2,512,4]{1,2,0:T(4,128)}, u32[]{:S(2)}) copy-start(f32[2,512,4]{1,2,0:T(4,128)} %copy-done.8) | copy-start | bytes 49156
  38.9 3.4 %copy-start.16 = (f32[4]{0:T(128)S(1)}, f32[4]{0:T(128)}, u32[]{:S(2)}) copy-start(f32[4]{0:T(128)} %param.17) | copy-start | bytes 52
  38.9 3.5 %copy-start.10 = (f32[6,512]{1,0:T(8,128)S(1)}, f32[6,512]{1,0:T(8,128)}, u32[]{:S(2)}) copy-start(f32[6,512]{1,0:T(8,128)} %fusion.62) | copy-start | bytes 36868
  42.1 2.7 copy-start.15
  42.1 6.7 %copy-start.3 = (bf16[512,1024]{1,0:T(8,128)(2,1)S(1)}, bf16[512,1024]{1,0:T(8,128)(2,1)}, u32[]{:S(2)}) copy-start(bf16[512,1024]{1,0:T(8,128)(2,1)} %all-gather.5.cloned.1.call-done) | copy-start | bytes 3145732
  50.9 156.8 %copy-start.17 = (s32[1,6]{1,0:T(1,128)S(1)}, s32[1,6]{1,0:T(1,128)}, u32[]{:S(2)}) copy-start(s32[1,6]{1,0:T(1,128)} %param.22) | copy-start | bytes 76
  239.8 2.1 copy-start.5
  239.8 2.1 copy-start.6
  239.8 2.0 copy-start.11
  239.8 2.0 copy-start.12
  241.9 4.1 %copy-start.13 = (f32[512,4]{0,1:T(4,128)S(1)}, f32[512,4]{0,1:T(4,128)}, u32[]{:S(2)}) copy-start(f32[512,4]{0,1:T(4,128)} %fusion.69) | copy-start | bytes 24580
  246.0 3.1 copy-start.4
  251.2 12.5 %copy-start.2 = (bf16[256,1024]{1,0:T(8,128)(2,1)S(1)}, bf16[256,1024]{1,0:T(8,128)(2,1)}, u32[]{:S(2)}) copy-start(bf16[256,1024]{1,0:T(8,128)(2,1)} %param.13) | copy-start | bytes 1572868
  251.2 50.4 %copy-start.14 = (f32[1,1024]{1,0:T(1,128)S(1)}, f32[1,1024]{1,0:T(1,128)}, u32[]{:S(2)}) copy-start(f32[1,1024]{1,0:T(1,128)} %get-tuple-element.27) | copy-start | bytes 12292
  251.2 50.4 %all-gather.11.cloned.1.call-start = ((), (), s32[]{:S(2)}) async-start(), calls=%async_computation.5 | async-start | bytes 25952256 | tf_op jit(solution)/shard_map/all_gather | solution.py:124
  265.1 36.5 %copy-start.7 = (bf16[256,1024]{1,0:T(8,128)(2,1)}, bf16[256,1024]{1,0:T(8,128)(2,1)S(1)}, u32[]{:S(2)}) copy-start(bf16[256,1024]{1,0:T(8,128)(2,1)S(1)} %get-tuple-element.24) | copy-start | bytes 1572868
  307.7 5.4 %copy-start.1 = (bf16[3,1024,512]{2,1,0:T(8,128)(2,1)S(1)}, bf16[3,1024,512]{2,1,0:T(8,128)(2,1)}, u32[]{:S(2)}) copy-start(bf16[3,1024,512]{2,1,0:T(8,128)(2,1)} %param.15) | copy-start | bytes 9437188
Sparse Core Ops, SparseCore 0:
  11.5 15.3 all-gather.4
  28.5 14.6 all-gather.6
  46.0 161.6 all-gather.8
  251.3 12.3 reduce-scatter.1
  265.3 36.2 all-gather.10
where the time goes:
time: 320 us
  waiting for transfers between devices  211 us (66%)
  matrix products  72.2 us (23%)
  other arithmetic  14.3 us (4%)
  between operations  13.4 us (4%)
  local copies, waits for them, and re-layouts  8.44 us (3%)
    all_gather x1, waiting for transfers between devices, on_device(): token_segment = lax.all_gather(caches, 'req', axis=0, tiled=True)  152 us
    all_gather x1, waiting for transfers between devices, on_device(): lax.all_gather(feedforward_weight, 'col', axis=2, tiled=True)  36.4 us
    dot_general x1, matrix products, on_device(): jnp.einsum('sn,nhij->shij', select, token_segment, preferred_element_type...  32 us
    reduce_scatter x1, waiting for transfers between devices, on_device(): lax.psum_scatter(jnp.dot(head_out, head_output_weight, preferred_element_...  11.9 us
    all_gather x1, waiting for transfers between devices, on_device(): gathered = lax.all_gather(normalized_rows, 'col', axis=0, tiled=True)  8.81 us
  transfers between devices with their start and end apart: 5, of which 4 were waited for; matrix products, arithmetic and copies ran while one was open for 11% of the time, Pallas kernels for 0%

commit v1 on v0

--- a/solution.py
+++ b/solution.py
@@ -37,7 +37,9 @@
     group_lengths = lengths[0].reshape(-1)
     scale = 1.0 / math.sqrt(head_size)
     normalized_rows = rms_scale(tokens, norm_gain_pair[0])
-    gathered = lax.all_gather(normalized_rows, "col", axis=0, tiled=True)
+    gathered = jnp.concatenate(
+        lax.all_to_all(jnp.stack([normalized_rows] * lax.axis_size("col")), "col", 0, 0), axis=0
+    )
     positions = jnp.arange(group, dtype=jnp.int32)
     ends = jnp.cumsum(group_lengths)
     starts = ends - group_lengths

time: 320 us -> 303 us (0.947)
  waiting for transfers between devices: 211 us -> 196 us
  starting transfers between devices: 0.16 us -> 5.95 us
  other arithmetic: 14.3 us -> 8.95 us
  local copies, waits for them, and re-layouts: 8.44 us -> 3.95 us
    all_gather x1 -> x0, waiting for transfers between devices: 8.81 us -> none  [on_device(): gathered = lax.all_gather(normalized_rows, 'col', axis=0, tiled=True)]
    all_gather x1, waiting for transfers between devices: 152 us -> 144 us  [on_device(): token_segment = lax.all_gather(caches, 'req', axis=0, tiled=True)]
    all_to_all x0 -> x1, starting transfers between devices: none -> 5.83 us  [on_device(): lax.all_to_all(jnp.stack([normalized_rows] * lax.axis_size('col')), 'col'...]
where the time goes in v1:
time: 303 us
  waiting for transfers between devices  196 us (65%)
  matrix products  74.5 us (25%)
  between operations  13.4 us (4%)
  other arithmetic  8.95 us (3%)
  starting transfers between devices  5.95 us (2%)
  local copies, waits for them, and re-layouts  3.95 us (1%)
    all_gather x1, waiting for transfers between devices, on_device(): token_segment = lax.all_gather(caches, 'req', axis=0, tiled=True)  144 us
    all_gather x1, waiting for transfers between devices, on_device(): lax.all_gather(feedforward_weight, 'col', axis=2, tiled=True)  36.4 us
    dot_general x1, matrix products, on_device(): jnp.einsum('sn,nhij->shij', select, token_segment, preferred_element_type...  32 us
    reduce_scatter x1, waiting for transfers between devices, on_device(): lax.psum_scatter(jnp.dot(head_out, head_output_weight, preferred_element_...  11.9 us
    dot_general x1, matrix products, on_device(): jnp.einsum('td,kdf->ktf', normed_two, token_segment[:2], preferred_elemen...  6.11 us
  transfers between devices with their start and end apart: 5, of which 4 were waited for; matrix products, arithmetic and copies ran while one was open for 11% of the time, Pallas kernels for 0%

profile of v1, /device:TPU:1, one launch (start us, length us, event | category | flops | bytes accessed | tf_op | source)
XLA Modules:
  0.0 302.5 jit_solution(2088774528153876671)
XLA Ops:
  6.6 0.7 all-gather.4.cloned.1.call-update
  7.3 0.7 all-gather.6.cloned.1.call-update
  8.0 1.2 fusion.38
  9.3 1.4 fusion.86
  10.6 1.2 fusion.50
  11.9 1.1 pad_maximum_fusion
  12.9 5.8 %all-to-all-start = ((bf16[2,256,1024]{2,1,0:T(8,128)(2,1)}), bf16[2,256,1024]{2,1,0:T(8,128)(2,1)}, u32[]{:S(2)}, u32[]{:S(2)}) async-start(bf16[2,256,1024]{2,1,0:T(8,128)(2,1)} %pad_maximum_fusion), calls=%async_computation | async-start | bytes 2097152 | tf_op jit(solution)/shard_map/all_to_all | solution.py:41
  18.9 1.7 all-to-all-done
  20.6 1.7 convolution_bitcast_fusion.1
  22.5 1.2 reduce-window.18
  24.1 0.6 copy.88
  24.7 4.2 %fusion.87 = (bf16[3,512,512]{1,2,0:T(8,128)(2,1)}, f32[3,512,512]{1,2,0:T(8,128)S(1)}) fusion(bf16[512,1024,1]{1,0,2:T(8,128)(2,1)} %bitcast.3, bf16[3,1024,512]{2,1,0:T(8,128)(2,1)S(1)} %copy-done), kind=kOutput, calls=%fused_computation.113 | convolution fusion | flops 1611399168 | bytes 8912896 | tf_op jit(solution)/shard_map/td,kdc->ktc/dot_general | solution.py:50
  29.7 0.6 fusion.68
  30.3 0.6 fusion.69
  31.1 2.4 convolution_convert_fusion
  33.6 1.0 fusion.85
  34.6 3.9 %fusion.35 = bf16[6,1024,16]{1,0,2:T(8,128)(2,1)S(1)} fusion(bf16[64,1024,16]{1,2,0:T(8,128)(2,1)} %all-gather.4.cloned.1.call-done, s32[6]{0:T(128)S(1)} %bitcast.135), kind=kOutput, calls=%fused_computation.41 | convolution fusion | flops 12681600 | bytes 2293784 | tf_op jit(solution)/shard_map/sa,adr->sdr/dot_general | solution.py:56
  38.6 1.7 fusion.91
  40.4 1.0 multiply_reduce_fusion
  42.0 4.8 %fusion.88 = (f32[4,512]{1,0:T(4,128)S(1)}, f32[4,512,512]{1,2,0:T(8,128)}) fusion(pred[512,512]{0,1:T(8,128)(4,1)S(1)} %fusion.46, bf16[512,4,128]{0,2,1:T(8,128)(2,1)S(1)} %add_convert_fusion, bf16[512,4,128]{0,2,1:T(8,128)(2,1)} %bitcast.128), kind=kOutput, calls=%fused_computation.114 | convolution fusion | flops 272630272 | bytes 5513216 | tf_op jit(solution)/shard_map/while/body/eval_jaxpr/sub | solution.py:105
  46.7 143.8 %all-gather.6.cloned.1.call-done = bf16[256,4,128,128]{3,2,1,0:T(8,128)(2,1)} async-done(((bf16[4,4,128,128]{3,2,1,0:T(8,128)(2,1)}), bf16[256,4,128,128]{3,2,1,0:T(8,128)(2,1)}) %all-gather.6.cloned.1.call-update) | async-done | bytes 33554448 | tf_op jit(solution)/shard_map/all_gather | solution.py:86
  190.6 32.0 %fusion.20 = bf16[6,4,128,128]{3,0,2,1:T(8,128)(2,1)S(1)} fusion(bf16[256,4,128,128]{3,2,1,0:T(8,128)(2,1)} %all-gather.6.cloned.1.call-done, s32[6]{0:T(128)S(1)} %bitcast.138), kind=kOutput, calls=%fused_computation.33 | convolution fusion | flops 201721344 | bytes 34340888 | tf_op jit(solution)/shard_map/sn,nhij->shij/dot_general | solution.py:89
  222.7 2.0 fusion.5
  224.7 4.1 %multiply_reduce_fusion.1 = (f32[512,4]{0,1:T(4,128)S(1)}, f32[512,4,128]{0,2,1:T(8,128)}) fusion(f32[512,4,128]{0,2,1:T(8,128)} %fusion.5, f32[512,4]{0,1:T(4,128)S(1)} %copy-done.9, bf16[512,4,128]{0,2,1:T(8,128)(2,1)S(1)} %bitcast.126, f32[4,512]{1,0:T(4,128)S(1)} %bitcast.132, pred[512,512]{0,1:T(8,128)(4,1)S(1)} %fusion.46, ...), kind=kOutput, calls=%fused_computation.53 | convolution fusion | flops 543160320 | bytes 3956736 | tf_op jit(solution)/shard_map/while/body/eval_jaxpr/hqk,khd->qhd/dot_general | solution.py:110
  228.8 3.1 %fusion.31 = bf16[512,4,128]{0,2,1:T(8,128)(2,1)S(1)} fusion(bf16[512,4,128]{0,2,1:T(8,128)(2,1)S(1)} %bitcast.127, f32[4,512,512]{1,2,0:T(8,128)} %get-tuple-element.44, f32[4,512]{1,0:T(4,128)S(1)} %get-tuple-element.42, f32[512,4,128]{0,2,1:T(8,128)} %get-tuple-element.46, f32[512,4]{0,1:T(4,128)S(1)} %add_rsqrt_fusion, f32[512,4]{0,1:T(4,128)S(1)} %copy-done.11), kind=kOutput, calls=%fused_computation.39 | convolution fusion | flops 271581184 | bytes 6316032 | tf_op jit(solution)/shard_map/while/body/eval_jaxpr/hqk,khd->qhd/dot_general | solution.py:107
  232.0 2.1 fusion.92
  234.1 0.5 all-gather.8.cloned.1.call-update
  234.7 11.9 %reduce-scatter.2.cloned.1.call-done = f32[256,1024]{1,0:T(8,128)} async-done(((f32[512,1024]{1,0:T(8,128)}), f32[256,1024]{1,0:T(8,128)}) %reduce-scatter.2.cloned.1.call-update) | async-done | bytes 1048592 | tf_op jit(solution)/shard_map/reduce_scatter | solution.py:118
  246.6 1.5 fusion.42
  248.1 36.4 %all-gather.8.cloned.1.call-done = bf16[3,1024,2816]{2,1,0:T(8,128)(2,1)} async-done(((bf16[3,1024,1408]{2,1,0:T(8,128)(2,1)}), bf16[3,1024,2816]{2,1,0:T(8,128)(2,1)}) %all-gather.8.cloned.1.call-update) | async-done | bytes 17301520 | tf_op jit(solution)/shard_map/all_gather | solution.py:126
  284.5 6.1 %fusion.7 = f32[2,256,2816]{2,1,0:T(8,128)S(1)} fusion(bf16[3,1024,2816]{2,1,0:T(8,128)(2,1)} %all-gather.8.cloned.1.call-done, bf16[256,1024]{1,0:T(8,128)(2,1)S(1)} %get-tuple-element.24, f32[1024]{0:T(1024)S(1)} %bitcast.133, f32[256]{0:T(256)S(1)} %add_rsqrt_fusion.1), kind=kOutput, calls=%fused_computation.10 | convolution fusion | flops 2953838592 | bytes 17830912 | tf_op jit(solution)/shard_map/td,kdf->ktf/dot_general | solution.py:127
  290.6 5.4 %fusion.32 = bf16[256,1024]{1,0:T(8,128)(2,1)} fusion(bf16[3,1024,2816]{2,1,0:T(8,128)(2,1)} %all-gather.8.cloned.1.call-done, f32[2,256,2816]{2,1,0:T(8,128)S(1)} %fusion.7, bf16[256,1024]{1,0:T(8,128)(2,1)} %copy-done.7), kind=kOutput, calls=%fused_computation.40 | convolution fusion | flops 1481506816 | bytes 12582912 | tf_op jit(solution)/shard_map/tf,df->td/dot_general | solution.py:131
  (64 shorter events, 2.6 us)
Async XLA Ops:
  6.5 18.2 %copy-start = (bf16[3,1024,512]{2,1,0:T(8,128)(2,1)S(1)}, bf16[3,1024,512]{2,1,0:T(8,128)(2,1)}, u32[]{:S(2)}) copy-start(bf16[3,1024,512]{2,1,0:T(8,128)(2,1)} %param.15) | copy-start | bytes 9437188
  6.5 12.2 %copy-start.16 = (s32[1,2,3]{2,1,0:T(2,128)S(1)}, s32[1,2,3]{2,1,0:T(2,128)}, u32[]{:S(2)}) copy-start(s32[1,2,3]{2,1,0:T(2,128)} %param.20) | copy-start | bytes 76
  6.5 14.1 %copy-start.8 = (bf16[2,1024,4]{1,2,0:T(4,128)(2,1)S(1)}, bf16[2,1024,4]{1,2,0:T(4,128)(2,1)}, u32[]{:S(2)}) copy-start(bf16[2,1024,4]{1,2,0:T(4,128)(2,1)} %param.16) | copy-start | bytes 49156
  6.5 15.8 %copy-start.14 = (f32[4]{0:T(128)S(1)}, f32[4]{0:T(128)}, u32[]{:S(2)}) copy-start(f32[4]{0:T(128)} %param.17) | copy-start | bytes 52
  6.5 28.1 %all-gather.4.cloned.1.call-start = ((), (), s32[]{:S(2)}) async-start(), calls=%async_computation.2 | async-start | bytes 3145728 | tf_op jit(solution)/shard_map/all_gather | solution.py:53
  7.3 183.3 %all-gather.6.cloned.1.call-start = ((), (), s32[]{:S(2)}) async-start(), calls=%async_computation.3 | async-start | bytes 34078720 | tf_op jit(solution)/shard_map/all_gather | solution.py:86
  12.9 7.7 %all-to-all-start = ((bf16[2,256,1024]{2,1,0:T(8,128)(2,1)}), bf16[2,256,1024]{2,1,0:T(8,128)(2,1)}, u32[]{:S(2)}, u32[]{:S(2)}) async-start(bf16[2,256,1024]{2,1,0:T(8,128)(2,1)} %pad_maximum_fusion), calls=%async_computation | async-start | bytes 2097152 | tf_op jit(solution)/shard_map/all_to_all | solution.py:41
  18.8 227.8 %reduce-scatter.2.cloned.1.call-start = ((), (), s32[]{:S(2)}) async-start(), calls=%async_computation.4 | async-start | bytes 3145728 | tf_op jit(solution)/shard_map/reduce_scatter | solution.py:118
  28.9 4.6 %copy-start.4 = (bf16[3,512,512]{1,2,0:T(8,128)(2,1)S(1)}, bf16[3,512,512]{1,2,0:T(8,128)(2,1)}, u32[]{:S(2)}) copy-start(bf16[3,512,512]{1,2,0:T(8,128)(2,1)} %get-tuple-element.29) | copy-start | bytes 4718596
  28.9 5.7 %copy-start.13 = (s32[1,6]{1,0:T(1,128)S(1)}, s32[1,6]{1,0:T(1,128)}, u32[]{:S(2)}) copy-start(s32[1,6]{1,0:T(1,128)} %param.21) | copy-start | bytes 76
  42.0 148.6 %copy-start.15 = (s32[1,6]{1,0:T(1,128)S(1)}, s32[1,6]{1,0:T(1,128)}, u32[]{:S(2)}) copy-start(s32[1,6]{1,0:T(1,128)} %param.22) | copy-start | bytes 76
  222.6 2.1 copy-start.5
  222.7 2.1 copy-start.6
  222.7 2.0 copy-start.9
  222.7 2.0 copy-start.10
  224.7 4.1 %copy-start.11 = (f32[512,4]{0,1:T(4,128)S(1)}, f32[512,4]{0,1:T(4,128)}, u32[]{:S(2)}) copy-start(f32[512,4]{0,1:T(4,128)} %fusion.68) | copy-start | bytes 24580
  228.8 3.1 %copy-start.3 = (bf16[512,1024]{1,0:T(8,128)(2,1)S(1)}, bf16[512,1024]{1,0:T(8,128)(2,1)}, u32[]{:S(2)}) copy-start(bf16[512,1024]{1,0:T(8,128)(2,1)} %param.24) | copy-start | bytes 3145732
  234.1 12.5 %copy-start.2 = (bf16[256,1024]{1,0:T(8,128)(2,1)S(1)}, bf16[256,1024]{1,0:T(8,128)(2,1)}, u32[]{:S(2)}) copy-start(bf16[256,1024]{1,0:T(8,128)(2,1)} %param.13) | copy-start | bytes 1572868
  234.1 50.4 %copy-start.12 = (f32[1,1024]{1,0:T(1,128)S(1)}, f32[1,1024]{1,0:T(1,128)}, u32[]{:S(2)}) copy-start(f32[1,1024]{1,0:T(1,128)} %get-tuple-element.27) | copy-start | bytes 12292
  234.1 50.4 %all-gather.8.cloned.1.call-start = ((), (), s32[]{:S(2)}) async-start(), calls=%async_computation.5 | async-start | bytes 25952256 | tf_op jit(solution)/shard_map/all_gather | solution.py:126
  248.0 36.4 %copy-start.7 = (bf16[256,1024]{1,0:T(8,128)(2,1)}, bf16[256,1024]{1,0:T(8,128)(2,1)S(1)}, u32[]{:S(2)}) copy-start(bf16[256,1024]{1,0:T(8,128)(2,1)S(1)} %get-tuple-element.24) | copy-start | bytes 1572868
  290.6 5.4 %copy-start.1 = (bf16[3,1024,512]{2,1,0:T(8,128)(2,1)S(1)}, bf16[3,1024,512]{2,1,0:T(8,128)(2,1)}, u32[]{:S(2)}) copy-start(bf16[3,1024,512]{2,1,0:T(8,128)(2,1)} %param.15) | copy-start | bytes 9437188
Sparse Core Ops, SparseCore 0:
  9.0 16.9 all-gather.3
  28.9 161.6 all-gather.5
  234.2 12.3 reduce-scatter.1
  248.2 36.2 all-gather.7
